TPU v7x, 256 devices: a whole 4x4x8 slice. The times are simulated.
256 devices in a mesh: row: 16 (over x, y_hi, core), col: 16 (over y_lo, z).
Axes of the slice: x: 4, y: 4 (y_hi: 2, y_lo: 2; y = y_hi * 2 + y_lo), z: 8, core: 2. Of those that a mesh axis runs over, the one named last changes fastest.
Arguments:
- left_rows: float32 [1024, 61440], P('col', 'row'), may hold values from -1.2 to 1.2
- right_cols: float32 [61440, 4096], P('col', 'row'), may hold values from -1.2 to 1.2
- left_pattern: int32 [16, 240], replicated, may hold values from 0 to 1, as said below
- right_pattern: int32 [240, 16], replicated, may hold values from 0 to 1, as said below
Outputs:
- square_terms: float32 [1024, 4096], P('col', 'row')
Inputs may be any that keep to these rules, and one draw needn't show every extreme that they name: Every device's tile of left_pattern (row b, inner blocks from a * 15) has between 1 and 3 occupied blocks, and some tile has exactly 3 in every draw. Every device's tile of right_pattern (inner blocks from b * 15, column a) has between 1 and 3 occupied blocks, and some tile has exactly 3 in every draw.
All inputs are finite; a program needn't handle non-finite values.
Results may differ from a plain program's by a relative error of at most 0.0001.
Values sent between devices are 32-bit elements; how exact they have to be, the bound alone decides.
No kernel may reach another device: no remote copies, remote signals or barrier semaphores. Data moves between devices by JAX's collectives and lax.ppermute only.
A program may use at most 128 MiB of HBM per device.

v0:
```python
import jax
import jax.numpy as jnp
from jax import lax
from jax.sharding import PartitionSpec as P

STEPS = 4


def from_behind(value, axis, steps):
    count = lax.axis_size(axis)
    pairs = [(source, (source + steps) % count) for source in range(count)]
    return lax.ppermute(value, axis, pairs)


def spread(x, axis, root):
    mine = lax.axis_index(axis) == root
    return lax.psum(jnp.where(mine, x, jnp.zeros_like(x)), axis)


def left_flags(left_pattern, block_row, block_col, per_k):
    return lax.dynamic_slice(left_pattern, (block_row, block_col * per_k), (1, per_k)).reshape(-1)


def right_flags(right_pattern, block_row, block_col, trows):
    return lax.dynamic_slice(right_pattern, (block_row * trows, block_col), (trows, 1)).reshape(-1)


def body(left_rows, right_cols, left_pattern, right_pattern):
    nrow = lax.axis_size("row")
    ncol = lax.axis_size("col")
    ratio = nrow // ncol
    lrows, left_width = left_rows.shape
    right_height, blk = right_cols.shape
    per_k = left_width // blk
    trows = right_height // blk
    rowdev = lax.axis_index("row")
    coldev = lax.axis_index("col")
    own_left = left_flags(left_pattern, coldev, rowdev, per_k)
    own_right = right_flags(right_pattern, coldev, rowdev, trows)
    left_masked = (
        left_rows.reshape(lrows, per_k, blk) * own_left.astype(jnp.float32)[None, :, None]
    ).reshape(lrows, left_width)
    right_masked = (
        right_cols.reshape(trows, blk, blk) * own_right.astype(jnp.float32)[:, None, None]
    ).reshape(right_height, blk)
    total = jnp.zeros((lrows, blk), jnp.float32)
    highest = lax.Precision.HIGHEST
    right = right_masked
    for step in range(STEPS):
        if step > 0 and step % ratio == 0:
            right = from_behind(right, "col", -1)
        root = (coldev * ratio + step) % nrow
        left = spread(left_masked, "row", root)
        total = total + jnp.dot(left, right, precision=highest, preferred_element_type=jnp.float32)
    return total


def solution(mesh):
    return jax.shard_map(
        body,
        mesh=mesh,
        in_specs=(P("col", "row"), P("col", "row"), P(), P()),
        out_specs=P("col", "row"),
        check_vma=False,
    )
```

profile of v0, /device:TPU:1, one launch (start us, length us, event | category | flops | bytes accessed | tf_op | source)
XLA Modules:
  0.0 441.3 jit_solution(10440948626347398094)
XLA Ops:
  6.5 0.0 all-reduce.3.cloned.1.call-start
  6.5 0.8 convert_bitcast_fusion
  7.3 0.1 mul.38
  7.4 0.0 copy-start.4
  7.4 2.8 broadcast_multiply_fusion
  10.2 0.0 copy-start
  10.2 2.0 copy-done
  12.1 7.4 %collective-permute-start = (f32[3840,256]{1,0:T(8,128)S(1)}, f32[3840,256]{1,0:T(8,128)}, u32[]{:S(2)}, u32[]{:S(2)}) collective-permute-start(f32[3840,256]{1,0:T(8,128)S(1)} %broadcast_multiply_fusion), channel_id=1, source_target_pairs={{0,15},{1,0},{2,1},{3,2},{4,3},{5,4},{6,5},{7,6},{8,7},{9,8},{10,9... | collective-permute-start | bytes 11796488 | tf_op jit(solution)/shard_map/ppermute | solution.py:12
  19.5 83.6 %collective-permute-done = f32[3840,256]{1,0:T(8,128)} collective-permute-done((f32[3840,256]{1,0:T(8,128)S(1)}, f32[3840,256]{1,0:T(8,128)}, u32[]{:S(2)}, u32[]{:S(2)}) %collective-permute-start) | collective-permute-done | bytes 3932192 | tf_op jit(solution)/shard_map/ppermute | solution.py:12
  103.2 4.4 %collective-permute-start.1 = (f32[3840,256]{1,0:T(8,128)}, f32[3840,256]{1,0:T(8,128)}, u32[]{:S(2)}, u32[]{:S(2)}) collective-permute-start(f32[3840,256]{1,0:T(8,128)} %collective-permute-done), channel_id=1, source_target_pairs={{0,15},{1,0},{2,1},{3,2},{4,3},{5,4},{6,5},{7,6},{8,7},{9,8},{10,9... | collective-permute-start | bytes 11796488 | tf_op jit(solution)/shard_map/ppermute | solution.py:12
  107.6 0.8 convert_bitcast_fusion.1
  108.3 0.1 mul.33
  108.4 0.0 copy-done.4
  108.4 2.1 multiply_select_fusion
  110.5 0.0 all-reduce.3.cloned.1.call-update
  110.5 82.8 %collective-permute-done.1 = f32[3840,256]{1,0:T(8,128)} collective-permute-done((f32[3840,256]{1,0:T(8,128)}, f32[3840,256]{1,0:T(8,128)}, u32[]{:S(2)}, u32[]{:S(2)}) %collective-permute-start.1) | collective-permute-done | bytes 3932192 | tf_op jit(solution)/shard_map/ppermute | solution.py:12
  193.4 4.3 collective-permute-start.2
  197.7 218.7 %all-reduce.3.cloned.1.call-done = (f32[64,3840]{1,0:T(8,128)}, f32[64,3840]{1,0:T(8,128)}, f32[64,3840]{1,0:T(8,128)}, f32[64,3840]{1,0:T(8,128)}) async-done(((f32[64,3840]{1,0:T(8,128)}, f32[64,3840]{1,0:T(8,128)}, f32[64,3840]{1,0:T(8,128)}, f32[64,3840]{1,0:T(8,128)}), (f32[64,3840]{1,0:T(8,128)}, f32[64,3840]{1,0:T(8,128)}, f32[64,3840]{1,0:T(8,128)}, ...) | async-done | bytes 3932176 | tf_op jit(solution)/shard_map/psum | solution.py:17
  416.3 0.0 copy-start.3
  416.4 0.0 copy-start.2
  416.4 4.6 %fusion = f32[64,256]{1,0:T(8,128)S(1)} fusion(f32[64,3840]{1,0:T(8,128)} %get-tuple-element.5, f32[3840,256]{1,0:T(8,128)} %copy-done), kind=kOutput, calls=%fused_computation.10 | convolution fusion | flops 754974720 | bytes 4980736 | tf_op jit(solution)/shard_map/dot_general | solution.py:54
  421.0 0.0 copy-done.3
  421.0 0.0 copy-start.1
  421.0 4.3 convolution_add_fusion.2
  425.3 0.0 copy-done.2
  425.3 4.2 convolution_add_fusion.1
  429.6 0.0 collective-permute-done.2
  429.6 0.0 copy-done.1
  429.6 4.9 %convolution_add_fusion = f32[64,256]{1,0:T(8,128)} fusion(f32[64,256]{1,0:T(8,128)S(1)} %convolution_add_fusion.1, f32[64,3840]{1,0:T(8,128)S(1)} %copy-done.1, f32[3840,256]{1,0:T(8,128)} %collective-permute-done.2), kind=kOutput, calls=%fused_computation.1 | convolution fusion | flops 754991104 | bytes 5046272 | tf_op jit(solution)/shard_map/dot_general | solution.py:54
  (2 shorter events, 0.0 us)
Async XLA Ops:
  6.5 409.8 %all-reduce.3.cloned.1.call-start = ((), (), s32[]{:S(2)}) async-start(), calls=%async_computation | async-start | bytes 7864320 | tf_op jit(solution)/shard_map/psum | solution.py:17
  7.4 101.0 %copy-start.4 = (f32[64,3840]{1,0:T(8,128)S(1)}, f32[64,3840]{1,0:T(8,128)}, u32[]{:S(2)}) copy-start(f32[64,3840]{1,0:T(8,128)} %param.4) | copy-start | bytes 2949124
  10.2 2.0 copy-start
  12.1 91.0 %collective-permute-start = (f32[3840,256]{1,0:T(8,128)S(1)}, f32[3840,256]{1,0:T(8,128)}, u32[]{:S(2)}, u32[]{:S(2)}) collective-permute-start(f32[3840,256]{1,0:T(8,128)S(1)} %broadcast_multiply_fusion), channel_id=1, source_target_pairs={{0,15},{1,0},{2,1},{3,2},{4,3},{5,4},{6,5},{7,6},{8,7},{9,8},{10,9... | collective-permute-start | bytes 11796488 | tf_op jit(solution)/shard_map/ppermute | solution.py:12
  103.2 90.2 %collective-permute-start.1 = (f32[3840,256]{1,0:T(8,128)}, f32[3840,256]{1,0:T(8,128)}, u32[]{:S(2)}, u32[]{:S(2)}) collective-permute-start(f32[3840,256]{1,0:T(8,128)} %collective-permute-done), channel_id=1, source_target_pairs={{0,15},{1,0},{2,1},{3,2},{4,3},{5,4},{6,5},{7,6},{8,7},{9,8},{10,9... | collective-permute-start | bytes 11796488 | tf_op jit(solution)/shard_map/ppermute | solution.py:12
  193.4 236.2 %collective-permute-start.2 = (f32[3840,256]{1,0:T(8,128)}, f32[3840,256]{1,0:T(8,128)}, u32[]{:S(2)}, u32[]{:S(2)}) collective-permute-start(f32[3840,256]{1,0:T(8,128)} %collective-permute-done.1), channel_id=1, source_target_pairs={{0,15},{1,0},{2,1},{3,2},{4,3},{5,4},{6,5},{7,6},{8,7},{9,8},{10,9... | collective-permute-start | bytes 11796488 | tf_op jit(solution)/shard_map/ppermute | solution.py:12
  416.3 4.7 %copy-start.3 = (f32[64,3840]{1,0:T(8,128)S(1)}, f32[64,3840]{1,0:T(8,128)}, u32[]{:S(2)}) copy-start(f32[64,3840]{1,0:T(8,128)} %get-tuple-element.6) | copy-start | bytes 2949124
  416.4 9.0 %copy-start.2 = (f32[64,3840]{1,0:T(8,128)S(1)}, f32[64,3840]{1,0:T(8,128)}, u32[]{:S(2)}) copy-start(f32[64,3840]{1,0:T(8,128)} %get-tuple-element.7) | copy-start | bytes 2949124
  421.0 8.6 %copy-start.1 = (f32[64,3840]{1,0:T(8,128)S(1)}, f32[64,3840]{1,0:T(8,128)}, u32[]{:S(2)}) copy-start(f32[64,3840]{1,0:T(8,128)} %get-tuple-element.8) | copy-start | bytes 2949124
Sparse Core Ops, SparseCore 0:
  110.6 305.6 all-reduce.2
where the time goes:
time: 442 us; the launch traced here: 441 us
  waiting for transfers between devices  385 us (87%)
  matrix products  18.1 us (4%)
  starting transfers between devices  16.1 us (4%)
  between operations  13.5 us (3%)
  other arithmetic  6.37 us (1%)
    psum x1, waiting for transfers between devices, spread(): return lax.psum(jnp.where(mine, x, jnp.zeros_like(x)), axis)  219 us
    ppermute x3, waiting for transfers between devices, from_behind(): return lax.ppermute(value, axis, pairs)  166 us
    dot_general x4, matrix products, body(): jnp.dot(left, right, precision=highest, preferred_element_type=jnp.float32)  18.1 us
    ppermute x3, starting transfers between devices, from_behind(): return lax.ppermute(value, axis, pairs)  16.1 us
  transfers between devices with their start and end apart: 4, of which 3 were waited for; matrix products, arithmetic and copies ran while one was open for 4% of the time, Pallas kernels for 0%

commit v1 on v0

v1 whole, which is shorter than its diff:
```python
import jax
import jax.numpy as jnp
from jax import lax
from jax.sharding import PartitionSpec as P

STEPS = 4
CAP = 3


def from_behind(value, axis, steps):
    count = lax.axis_size(axis)
    pairs = [(source, (source - steps) % count) for source in range(count)]
    return lax.ppermute(value, axis, pairs)


def occupied(flags, cap):
    flags = flags != 0
    rank = jnp.cumsum(flags.astype(jnp.int32)) - 1
    where = jnp.arange(flags.shape[0], dtype=jnp.int32)
    hit = flags[None, :] & (rank[None, :] == jnp.arange(cap, dtype=jnp.int32)[:, None])
    index = jnp.sum(jnp.where(hit, where[None, :], 0), axis=1)
    return index, jnp.any(hit, axis=1)


def left_flags(left_pattern, block_row, block_col, per_k):
    return lax.dynamic_slice(left_pattern, (block_row, block_col * per_k), (1, per_k)).reshape(-1)


def right_flags(right_pattern, block_row, block_col, trows):
    return lax.dynamic_slice(right_pattern, (block_row * trows, block_col), (trows, 1)).reshape(-1)


def pick_cols(x, index, blk):
    return jnp.concatenate(
        [lax.dynamic_slice_in_dim(x, index[s] * blk, blk, axis=1) for s in range(index.shape[0])], axis=1
    )


def pick_rows(x, index, blk):
    return jnp.concatenate(
        [lax.dynamic_slice_in_dim(x, index[s] * blk, blk, axis=0) for s in range(index.shape[0])], axis=0
    )


def body(left_rows, right_cols, left_pattern, right_pattern):
    nrow = lax.axis_size("row")
    ncol = lax.axis_size("col")
    ratio = nrow // ncol
    lrows, left_width = left_rows.shape
    right_height, blk = right_cols.shape
    per_k = left_width // blk
    trows = right_height // blk
    rowdev = lax.axis_index("row")
    coldev = lax.axis_index("col")

    own_left, _ = occupied(left_flags(left_pattern, coldev, rowdev, per_k), CAP)
    own_right, _ = occupied(right_flags(right_pattern, coldev, rowdev, trows), CAP)
    left_small = pick_cols(left_rows, own_left, blk)
    right_small = pick_rows(right_cols, own_right, blk)

    roots = [(coldev * ratio + step) % nrow for step in range(STEPS)]
    slots = jnp.stack([jnp.where(rowdev == root, left_small, jnp.zeros_like(left_small)) for root in roots])
    lefts = lax.psum(slots, "row")

    total = jnp.zeros((lrows, blk), jnp.float32)
    highest = lax.Precision.HIGHEST
    for step in range(STEPS):
        shift = step // ratio
        right = right_small if shift == 0 else from_behind(right_small, "col", shift)
        panel = roots[step]
        lidx, lok = occupied(left_flags(left_pattern, coldev, panel, per_k), CAP)
        ridx, rok = occupied(right_flags(right_pattern, (coldev + shift) % ncol, rowdev, trows), CAP)
        match = ((lidx[:, None] == ridx[None, :]) & lok[:, None] & rok[None, :]).astype(jnp.float32)
        left = lefts[step]
        blocks = [left[:, i * blk:(i + 1) * blk] for i in range(CAP)]
        aligned = []
        for j in range(CAP):
            part = match[0, j] * blocks[0]
            for i in range(1, CAP):
                part = part + match[i, j] * blocks[i]
            aligned.append(part)
        aligned = jnp.concatenate(aligned, axis=1)
        total = total + jnp.dot(aligned, right, precision=highest, preferred_element_type=jnp.float32)
    return total


def solution(mesh):
    return jax.shard_map(
        body,
        mesh=mesh,
        in_specs=(P("col", "row"), P("col", "row"), P(), P()),
        out_specs=P("col", "row"),
        check_vma=False,
    )
```

time: 442 us -> 218 us (0.49)
  waiting for transfers between devices: 385 us -> 151 us
  other arithmetic: 6.37 us -> 29.2 us
  matrix products: 18.1 us -> 3.81 us
  starting transfers between devices: 16.1 us -> 9.09 us
  local copies, waits for them, and re-layouts: 2.13 us -> 7.4 us
    ppermute x3, waiting for transfers between devices: 166 us -> 0.01 us  [from_behind(): return lax.ppermute(value, axis, pairs)]
    psum x1, waiting for transfers between devices: 219 us -> 151 us  [body(): lefts = lax.psum(slots, 'row')]
    add x0 -> x4, other arithmetic: none -> 22.6 us  [body(): part = part + match[i, j] * blocks[i]]
    dot_general x4, matrix products: 18.1 us -> 3.81 us  [body(): jnp.dot(aligned, right, precision=highest, preferred_element_type=jnp.flo...]
    ppermute x3, starting transfers between devices: 16.1 us -> 9.08 us  [from_behind(): return lax.ppermute(value, axis, pairs)]
  transfers between devices with their start and end apart: 4 -> 4, of which waited for: 3 -> 1; matrix products, arithmetic and copies ran while one was open for 4% -> 16% of each run, Pallas kernels for 0% -> 0%
where the time goes in v1:
time: 218 us
  waiting for transfers between devices  151 us (69%)
  other arithmetic  29.2 us (13%)
  between operations  17.4 us (8%)
  starting transfers between devices  9.09 us (4%)
  local copies, waits for them, and re-layouts  7.4 us (3%)
  matrix products  3.81 us (2%)
    psum x1, waiting for transfers between devices, body(): lefts = lax.psum(slots, 'row')  151 us
    add x4, other arithmetic, body(): part = part + match[i, j] * blocks[i]  22.6 us
    ppermute x3, starting transfers between devices, from_behind(): return lax.ppermute(value, axis, pairs)  9.08 us
  transfers between devices with their start and end apart: 4, of which 1 were waited for; matrix products, arithmetic and copies ran while one was open for 16% of the time, Pallas kernels for 0%

profile of v1, /device:TPU:1, one launch (start us, length us, event | category | flops | bytes accessed | tf_op | source)
XLA Modules:
  0.0 217.5 jit_solution(2198795887849036355)
XLA Ops:
  6.5 0.0 all-reduce.2.cloned.1.call-start
  6.5 1.0 compare_bitcast_fusion.3
  7.5 0.2 reduce-window.82
  7.7 1.0 compare_bitcast_fusion.2
  8.7 0.2 reduce-window.83
  8.8 0.1 select_reduce_fusion.6
  9.0 0.7 fusion.55
  11.7 1.2 constant_dynamic-slice_fusion.2
  12.8 0.1 pad_maximum_fusion.1
  12.9 7.5 %collective-permute-start = (f32[768,256]{1,0:T(8,128)S(1)}, f32[768,256]{1,0:T(8,128)S(1)}, u32[]{:S(2)}, u32[]{:S(2)}) collective-permute-start(f32[768,256]{1,0:T(8,128)S(1)} %pad_maximum_fusion.1), channel_id=1, source_target_pairs={{0,15},{1,0},{2,1},{3,2},{4,3},{5,4},{6,5},{7,6},{8,7},{9,8},{10,9... | collective-permute-start | bytes 2359304 | tf_op jit(solution)/shard_map/ppermute | solution.py:13
  20.4 1.6 collective-permute-start.2
  22.0 0.0 collective-permute-start.1
  22.0 0.6 fusion.54
  24.6 0.9 dynamic-slice_bitcast_fusion.2
  25.5 0.1 broadcast_select_fusion.3
  25.6 0.9 pad_maximum_fusion
  26.5 0.0 all-reduce.2.cloned.1.call-update
  26.5 0.2 reduce-window.84
  26.7 0.2 reduce-window.80
  26.9 0.2 reduce-window.85
  27.1 0.2 reduce-window.81
  27.3 0.1 fusion.38
  27.5 0.2 select_reduce_fusion.4
  27.6 0.2 fusion.37
  27.8 0.2 select_reduce_fusion.8
  27.9 0.2 reduce-window.88
  28.1 0.2 reduce-window.86
  28.3 0.2 reduce-window.87
  28.5 0.2 reduce-window.89
  28.7 0.2 fusion.34
  28.9 0.2 select_reduce_fusion.2
  29.0 0.2 fusion.33
  29.2 0.1 and_convert_fusion.1
  29.3 0.7 fusion.50
  29.9 0.1 and_convert_fusion.2
  30.0 0.1 select_reduce_fusion
  30.2 0.7 fusion.51
  30.9 0.1 and_convert_fusion.3
  30.9 0.7 fusion.52
  31.6 0.1 and_convert_fusion
  31.7 0.7 fusion.53
  32.4 150.5 %all-reduce.2.cloned.1.call-done = f32[4,64,768]{2,1,0:T(8,128)} async-done(((f32[4,64,768]{2,1,0:T(8,128)}), f32[4,64,768]{2,1,0:T(8,128)}) %all-reduce.2.cloned.1.call-update) | async-done | bytes 786448 | tf_op jit(solution)/shard_map/psum | solution.py:63
  182.9 1.3 slice_bitcast_fusion.1
  184.2 5.5 %multiply_add_fusion.5 = (f32[64,256]{1,0:T(8,128)S(1)}, f32[64,256]{1,0:T(8,128)S(1)}, f32[64,256]{1,0:T(8,128)S(1)}) fusion(f32[64,768]{1,0:T(8,128)S(1)} %get-tuple-element.11, f32[]{:T(128)} %bitcast.52, f32[]{:T(128)} %bitcast.51, f32[]{:T(128)} %bitcast.49, f32[]{:T(128)} %bitcast.55, f32[]{:T(128)} %bitcast.54, f32[]{:T(128)} %bitcast.53, ...), kind=kLoop, calls=%fused_computation.41 | loop fusion | flops 245760 | bytes 393252 | tf_op jit(solution)/shard_map/add | solution.py:80
  189.7 5.8 %multiply_add_fusion.8 = (f32[64,256]{1,0:T(8,128)S(1)}, f32[64,256]{1,0:T(8,128)S(1)}, f32[64,256]{1,0:T(8,128)S(1)}) fusion(f32[64,768]{1,0:T(8,128)S(1)} %get-tuple-element.13, f32[]{:T(128)} %bitcast.37, f32[]{:T(128)} %bitcast.36, f32[]{:T(128)} %bitcast.34, f32[]{:T(128)} %bitcast.40, f32[]{:T(128)} %bitcast.39, f32[]{:T(128)} %bitcast.38, ...), kind=kLoop, calls=%fused_computation.44 | loop fusion | flops 245760 | bytes 393252 | tf_op jit(solution)/shard_map/add | solution.py:80
  195.5 5.7 %multiply_add_fusion.11 = (f32[64,256]{1,0:T(8,128)S(1)}, f32[64,256]{1,0:T(8,128)S(1)}, f32[64,256]{1,0:T(8,128)S(1)}) fusion(f32[64,768]{1,0:T(8,128)S(1)} %get-tuple-element.14, f32[]{:T(128)} %bitcast.17, f32[]{:T(128)} %bitcast.16, f32[]{:T(128)} %bitcast.5, f32[]{:T(128)} %bitcast.20, f32[]{:T(128)} %bitcast.19, f32[]{:T(128)} %bitcast.18, ...), kind=kLoop, calls=%fused_computation.47 | loop fusion | flops 245760 | bytes 393252 | tf_op jit(solution)/shard_map/add | solution.py:80
  201.2 0.5 fusion.1
  201.7 5.6 %multiply_add_fusion.2 = (f32[64,256]{1,0:T(8,128)S(1)}, f32[64,256]{1,0:T(8,128)S(1)}, f32[64,256]{1,0:T(8,128)S(1)}) fusion(f32[64,768]{1,0:T(8,128)S(1)} %get-tuple-element.12, f32[]{:T(128)} %bitcast.67, f32[]{:T(128)} %bitcast.66, f32[]{:T(128)} %bitcast.64, f32[]{:T(128)} %bitcast.70, f32[]{:T(128)} %bitcast.69, f32[]{:T(128)} %bitcast.68, ...), kind=kLoop, calls=%fused_computation.38 | loop fusion | flops 245760 | bytes 393252 | tf_op jit(solution)/shard_map/add | solution.py:80
  207.3 0.0 collective-permute-done.2
  207.4 1.6 fusion.17
  209.0 0.0 collective-permute-done
  209.0 0.5 convolution_add_fusion.1
  209.5 0.0 collective-permute-done.1
  209.5 1.1 fusion
  (10 shorter events, 0.1 us)
Async XLA Ops:
  6.5 176.3 %all-reduce.2.cloned.1.call-start = ((), (), s32[]{:S(2)}) async-start(), calls=%async_computation | async-start | bytes 1572864 | tf_op jit(solution)/shard_map/psum | solution.py:63
  12.9 196.1 %collective-permute-start = (f32[768,256]{1,0:T(8,128)S(1)}, f32[768,256]{1,0:T(8,128)S(1)}, u32[]{:S(2)}, u32[]{:S(2)}) collective-permute-start(f32[768,256]{1,0:T(8,128)S(1)} %pad_maximum_fusion.1), channel_id=1, source_target_pairs={{0,15},{1,0},{2,1},{3,2},{4,3},{5,4},{6,5},{7,6},{8,7},{9,8},{10,9... | collective-permute-start | bytes 2359304 | tf_op jit(solution)/shard_map/ppermute | solution.py:13
  20.4 187.0 %collective-permute-start.2 = (f32[768,256]{1,0:T(8,128)S(1)}, f32[768,256]{1,0:T(8,128)}, u32[]{:S(2)}, u32[]{:S(2)}) collective-permute-start(f32[768,256]{1,0:T(8,128)S(1)} %pad_maximum_fusion.1), channel_id=1, source_target_pairs={{0,13},{1,14},{2,15},{3,0},{4,1},{5,2},{6,3},{7,4},{8,5},{9,6},{10... | collective-permute-start | bytes 2359304 | tf_op jit(solution)/shard_map/ppermute | solution.py:13
  22.0 187.5 %collective-permute-start.1 = (f32[768,256]{1,0:T(8,128)S(1)}, f32[768,256]{1,0:T(8,128)S(1)}, u32[]{:S(2)}, u32[]{:S(2)}) collective-permute-start(f32[768,256]{1,0:T(8,128)S(1)} %pad_maximum_fusion.1), channel_id=1, source_target_pairs={{0,14},{1,15},{2,0},{3,1},{4,2},{5,3},{6,4},{7,5},{8,6},{9,7},{10,... | collective-permute-start | bytes 2359304 | tf_op jit(solution)/shard_map/ppermute | solution.py:13
Sparse Core Ops, SparseCore 0:
  26.7 156.1 all-reduce.1

commit v2 on v1

v2 whole, which is shorter than its diff:
```python
import jax
import jax.numpy as jnp
from jax import lax
from jax.sharding import PartitionSpec as P

STEPS = 4
CAP = 3
QUAD = 4


def shifted(value, axis, steps):
    count = lax.axis_size(axis)
    pairs = [(source, (source - steps) % count) for source in range(count)]
    return lax.ppermute(value, axis, pairs)


def occupied(flags, cap):
    flags = flags != 0
    rank = jnp.cumsum(flags.astype(jnp.int32)) - 1
    where = jnp.arange(flags.shape[0], dtype=jnp.int32)
    hit = flags[None, :] & (rank[None, :] == jnp.arange(cap, dtype=jnp.int32)[:, None])
    index = jnp.sum(jnp.where(hit, where[None, :], 0), axis=1)
    return index, jnp.any(hit, axis=1)


def left_flags(left_pattern, block_row, block_col, per_k):
    return lax.dynamic_slice(left_pattern, (block_row, block_col * per_k), (1, per_k)).reshape(-1)


def right_flags(right_pattern, block_row, block_col, trows):
    return lax.dynamic_slice(right_pattern, (block_row * trows, block_col), (trows, 1)).reshape(-1)


def pick_cols(x, index, blk):
    return jnp.concatenate(
        [lax.dynamic_slice_in_dim(x, index[s] * blk, blk, axis=1) for s in range(index.shape[0])], axis=1
    )


def pick_rows(x, index, blk):
    return jnp.concatenate(
        [lax.dynamic_slice_in_dim(x, index[s] * blk, blk, axis=0) for s in range(index.shape[0])], axis=0
    )


def aligned_left(left, lidx, lok, ridx, rok, blk):
    parts = []
    for j in range(ridx.shape[0]):
        hit = (lidx == ridx[j]) & lok & rok[j]
        source = jnp.sum(jnp.where(hit, jnp.arange(lidx.shape[0], dtype=jnp.int32), 0))
        block = lax.dynamic_slice_in_dim(left, source * blk, blk, axis=1)
        parts.append(jnp.where(jnp.any(hit), block, jnp.zeros_like(block)))
    return jnp.concatenate(parts, axis=1)


def broadcast_lefts(left_small, coldev, rowdev, nrow, ncol):
    spread = nrow // QUAD
    flat = ("row", "col")
    received = []
    for hop in range(1, spread):
        pairs = []
        for c in range(ncol):
            for k in range(STEPS):
                root = (c + k) % nrow
                pairs.append((root * ncol + c, ((root + QUAD * hop) % nrow) * ncol + c))
        received.append(lax.ppermute(left_small, flat, pairs))
    is_root = ((rowdev - coldev) % nrow) < STEPS
    held = received[0]
    for more in received[1:]:
        held = held + more
    held = jnp.where(is_root, left_small, held)
    mine = rowdev % QUAD
    tiles = [held]
    for flip in range(1, QUAD):
        pairs = [(r, (r // QUAD) * QUAD + ((r % QUAD) ^ flip)) for r in range(nrow)]
        tiles.append(lax.ppermute(held, "row", pairs))
    tiles = jnp.stack(tiles)
    lefts = []
    for k in range(STEPS):
        flip = ((coldev + k) % QUAD) ^ mine
        lefts.append(lax.dynamic_index_in_dim(tiles, flip, axis=0, keepdims=False))
    return lefts


def body(left_rows, right_cols, left_pattern, right_pattern):
    nrow = lax.axis_size("row")
    ncol = lax.axis_size("col")
    assert nrow == ncol and nrow % QUAD == 0 and STEPS <= QUAD
    lrows, left_width = left_rows.shape
    right_height, blk = right_cols.shape
    per_k = left_width // blk
    trows = right_height // blk
    rowdev = lax.axis_index("row")
    coldev = lax.axis_index("col")

    own_left, _ = occupied(left_flags(left_pattern, coldev, rowdev, per_k), CAP)
    own_right, rok = occupied(right_flags(right_pattern, coldev, rowdev, trows), CAP)
    left_small = pick_cols(left_rows, own_left, blk)
    right_small = pick_rows(right_cols, own_right, blk)

    lefts = broadcast_lefts(left_small, coldev, rowdev, nrow, ncol)

    highest = lax.Precision.HIGHEST
    total = None
    for step in range(STEPS):
        left = lefts[step] if step == 0 else shifted(lefts[step], "col", -step)
        owner = (coldev - step) % ncol
        lidx, lok = occupied(left_flags(left_pattern, owner, coldev, per_k), CAP)
        aligned = aligned_left(left, lidx, lok, own_right, rok, blk)
        part = jnp.dot(aligned, right_small, precision=highest, preferred_element_type=jnp.float32)
        part = part if step == 0 else shifted(part, "col", step)
        total = part if total is None else total + part
    return total


def solution(mesh):
    return jax.shard_map(
        body,
        mesh=mesh,
        in_specs=(P("col", "row"), P("col", "row"), P(), P()),
        out_specs=P("col", "row"),
        check_vma=False,
    )
```

time: 218 us -> 107 us (0.49)
  waiting for transfers between devices: 151 us -> 18.6 us
  starting transfers between devices: 9.09 us -> 32.5 us
  other arithmetic: 29.2 us -> 37 us
  between operations: 17.4 us -> 11.6 us
  local copies, waits for them, and re-layouts: 7.4 us -> 4.15 us
    psum x1 -> x0, waiting for transfers between devices: 151 us -> none  [body(): lefts = lax.psum(slots, 'row')]
    ppermute x3 -> x12, starting transfers between devices: 9.08 us -> 32.5 us  [the longest x6 20.4 us: shifted(): return lax.ppermute(value, axis, pairs)]
    add x4 -> x0, other arithmetic: 22.6 us -> none  [body(): part = part + match[i, j] * blocks[i]]
    ppermute x3 -> x12, waiting for transfers between devices: 0.01 us -> 18.6 us  [the longest x6 12.2 us: shifted(): return lax.ppermute(value, axis, pairs)]
    reduce_or x0 -> x4, other arithmetic: none -> 18 us  [aligned_left(): parts.append(jnp.where(jnp.any(hit), block, jnp.zeros_like(block)))]
    reduce_sum x0 -> x12, other arithmetic: none -> 7.65 us  [aligned_left(): jnp.sum(jnp.where(hit, jnp.arange(lidx.shape[0], dtype=jnp.int32), 0))]
    select_n x1 -> x5, other arithmetic: 0.06 us -> 7.64 us  [the longest x4 7.6 us: aligned_left(): parts.append(jnp.where(jnp.any(hit), block, jnp.zeros_like(block)))]
  transfers between devices with their start and end apart: 4 -> 12, of which waited for: 1 -> 4; matrix products, arithmetic and copies ran while one was open for 16% -> 37% of each run, Pallas kernels for 0% -> 0%
where the time goes in v2:
time: 107 us
  other arithmetic  37 us (35%)
  starting transfers between devices  32.5 us (30%)
  waiting for transfers between devices  18.6 us (17%)
  between operations  11.6 us (11%)
  local copies, waits for them, and re-layouts  4.15 us (4%)
  matrix products  2.68 us (3%)
    ppermute x6, starting transfers between devices, shifted(): return lax.ppermute(value, axis, pairs)  20.4 us
    reduce_or x4, other arithmetic, aligned_left(): parts.append(jnp.where(jnp.any(hit), block, jnp.zeros_like(block)))  18 us
    ppermute x6, waiting for transfers between devices, shifted(): return lax.ppermute(value, axis, pairs)  12.2 us
    ppermute x3, starting transfers between devices, broadcast_lefts(): received.append(lax.ppermute(left_small, flat, pairs))  7.83 us
    reduce_sum x12, other arithmetic, aligned_left(): jnp.sum(jnp.where(hit, jnp.arange(lidx.shape[0], dtype=jnp.int32), 0))  7.65 us
    select_n x4, other arithmetic, aligned_left(): parts.append(jnp.where(jnp.any(hit), block, jnp.zeros_like(block)))  7.6 us
    ppermute x3, waiting for transfers between devices, broadcast_lefts(): tiles.append(lax.ppermute(held, 'row', pairs))  6.41 us
    ppermute x3, starting transfers between devices, broadcast_lefts(): tiles.append(lax.ppermute(held, 'row', pairs))  4.33 us
  transfers between devices with their start and end apart: 12, of which 4 were waited for; matrix products, arithmetic and copies ran while one was open for 37% of the time, Pallas kernels for 0%

profile of v2, /device:TPU:1, one launch (start us, length us, event | category | flops | bytes accessed | tf_op | source)
XLA Modules:
  0.0 106.5 jit_solution(8457948534499551721)
XLA Ops:
  0.0 0.9 compare_bitcast_fusion.5
  0.9 0.2 reduce-window.50
  1.1 0.2 reduce-window.51
  1.3 0.1 select_reduce_fusion.2
  1.4 0.7 fusion.59
  4.1 0.9 constant_dynamic-slice_fusion.5
  5.0 5.2 %collective-permute-start.2 = (f32[64,768]{1,0:T(8,128)S(1)}, f32[64,768]{1,0:T(8,128)S(1)}, u32[]{:S(2)}, u32[]{:S(2)}) collective-permute-start(f32[64,768]{1,0:T(8,128)S(1)} %pad_maximum_fusion.2), channel_id=1, source_target_pairs={{0,192},{16,208},{32,224},{48,240},{17,209},{33,225},{49,241},{65,... | collective-permute-start | bytes 589832 | tf_op jit(solution)/shard_map/ppermute | solution.py:66
  10.3 1.3 %collective-permute-start.1 = (f32[64,768]{1,0:T(8,128)S(1)}, f32[64,768]{1,0:T(8,128)S(1)}, u32[]{:S(2)}, u32[]{:S(2)}) collective-permute-start(f32[64,768]{1,0:T(8,128)S(1)} %pad_maximum_fusion.2), channel_id=1, source_target_pairs={{0,128},{16,144},{32,160},{48,176},{17,145},{33,161},{49,177},{65,... | collective-permute-start | bytes 589832 | tf_op jit(solution)/shard_map/ppermute | solution.py:66
  11.6 1.3 %collective-permute-start = (f32[64,768]{1,0:T(8,128)S(1)}, f32[64,768]{1,0:T(8,128)S(1)}, u32[]{:S(2)}, u32[]{:S(2)}) collective-permute-start(f32[64,768]{1,0:T(8,128)S(1)} %pad_maximum_fusion.2), channel_id=1, source_target_pairs={{0,64},{16,80},{32,96},{48,112},{17,81},{33,97},{49,113},{65,129},... | collective-permute-start | bytes 589832 | tf_op jit(solution)/shard_map/ppermute | solution.py:66
  13.0 0.8 compare_bitcast_fusion.4
  13.8 0.2 reduce-window.49
  14.0 0.2 reduce-window.48
  14.1 0.1 fusion.34
  14.3 0.1 select_reduce_fusion.4
  14.4 0.2 fusion.33
  14.6 0.7 fusion.57
  17.1 0.2 reduce-window.52
  17.3 0.2 reduce-window.53
  17.5 0.1 fusion.31
  17.7 0.2 select_reduce_fusion
  17.8 0.7 fusion.58
  18.5 4.5 %fusion.54 = (pred[]{:T(512)}, pred[3]{0:T(512)(128)(4,1)S(1)}, pred[]{:T(512)}, pred[3]{0:T(512)(128)(4,1)S(1)}, pred[]{:T(512)}, /*index=5*/pred[3]{0:T(512)(128)(4,1)S(1)}) fusion(pred[]{:T(512)} %bitcast.6, pred[3]{0:T(512)(128)(4,1)S(1)} %get-tuple-element.93, s32[3]{0:T(128)S(1)} %get-tuple-element.87, s32[]{:T(128)} %bitcast.5, pred[]{:T(512)} %bitcast.22, ...), kind=kLoop, calls=%fused_computation.134 | loop fusion | flops 33 | bytes 42 | tf_op jit(solution)/shard_map/reduce_or | solution.py:52
  23.0 0.6 select_reduce_fusion.7
  24.2 0.6 select_reduce_fusion.6
  25.4 0.6 select_reduce_fusion.8
  26.6 4.5 %fusion.48 = (pred[]{:T(512)}, pred[3]{0:T(512)(128)(4,1)S(1)}, pred[]{:T(512)}, pred[3]{0:T(512)(128)(4,1)S(1)}, pred[]{:T(512)}, /*index=5*/pred[3]{0:T(512)(128)(4,1)S(1)}) fusion(pred[]{:T(512)} %bitcast.6, pred[3]{0:T(512)(128)(4,1)S(1)} %get-tuple-element.95, s32[3]{0:T(128)S(1)} %get-tuple-element.89, s32[]{:T(128)} %bitcast.5, pred[]{:T(512)} %bitcast.22, ...), kind=kLoop, calls=%fused_computation.128 | loop fusion | flops 33 | bytes 42 | tf_op jit(solution)/shard_map/reduce_or | solution.py:52
  31.1 0.7 select_reduce_fusion.13
  32.4 0.7 select_reduce_fusion.12
  33.7 0.7 select_reduce_fusion.14
  35.0 4.5 %fusion.51 = (pred[]{:T(512)}, pred[3]{0:T(512)(128)(4,1)S(1)}, pred[]{:T(512)}, pred[3]{0:T(512)(128)(4,1)S(1)}, pred[]{:T(512)}, /*index=5*/pred[3]{0:T(512)(128)(4,1)S(1)}) fusion(pred[]{:T(512)} %bitcast.6, pred[3]{0:T(512)(128)(4,1)S(1)} %get-tuple-element.94, s32[3]{0:T(128)S(1)} %get-tuple-element.88, s32[]{:T(128)} %bitcast.5, pred[]{:T(512)} %bitcast.22, ...), kind=kLoop, calls=%fused_computation.131 | loop fusion | flops 33 | bytes 42 | tf_op jit(solution)/shard_map/reduce_or | solution.py:52
  39.4 0.6 select_reduce_fusion.10
  40.6 0.6 select_reduce_fusion.9
  41.8 0.6 select_reduce_fusion.11
  43.1 4.5 %fusion.45 = (pred[]{:T(512)}, pred[3]{0:T(512)(128)(4,1)S(1)}, pred[]{:T(512)}, pred[3]{0:T(512)(128)(4,1)S(1)}, pred[]{:T(512)}, /*index=5*/pred[3]{0:T(512)(128)(4,1)S(1)}) fusion(pred[]{:T(512)} %bitcast.6, pred[3]{0:T(512)(128)(4,1)S(1)} %get-tuple-element.96, s32[3]{0:T(128)S(1)} %get-tuple-element.92, s32[]{:T(128)} %bitcast.5, pred[]{:T(512)} %bitcast.22, ...), kind=kLoop, calls=%fused_computation.125 | loop fusion | flops 33 | bytes 42 | tf_op jit(solution)/shard_map/reduce_or | solution.py:52
  47.6 0.0 collective-permute-done.2
  47.6 0.0 collective-permute-done.1
  47.6 0.0 collective-permute-done
  47.6 3.8 %collective-permute-start.5 = (f32[64,768]{1,0:T(8,128)S(1)}, f32[64,768]{1,0:T(8,128)S(1)}, u32[]{:S(2)}, u32[]{:S(2)}) collective-permute-start(f32[64,768]{1,0:T(8,128)S(1)} %add_select_fusion), channel_id=1, source_target_pairs={{0,48},{16,32},{32,16},{48,0},{64,112},{80,96},{96,80},{112,64},{1... | collective-permute-start | bytes 589832 | tf_op jit(solution)/shard_map/ppermute | solution.py:76
  51.4 0.1 collective-permute-start.4
  51.5 0.4 collective-permute-start.3
  51.9 0.6 select_reduce_fusion.16
  53.2 0.6 select_reduce_fusion.15
  54.5 2.4 %collective-permute-done.5 = f32[64,768]{1,0:T(8,128)S(1)} collective-permute-done((f32[64,768]{1,0:T(8,128)S(1)}, f32[64,768]{1,0:T(8,128)S(1)}, u32[]{:S(2)}, u32[]{:S(2)}) %collective-permute-start.5) | collective-permute-done | bytes 196640 | tf_op jit(solution)/shard_map/ppermute | solution.py:76
  56.9 4.0 %collective-permute-done.4 = f32[64,768]{1,0:T(8,128)S(1)} collective-permute-done((f32[64,768]{1,0:T(8,128)S(1)}, f32[64,768]{1,0:T(8,128)S(1)}, u32[]{:S(2)}, u32[]{:S(2)}) %collective-permute-start.4) | collective-permute-done | bytes 196640 | tf_op jit(solution)/shard_map/ppermute | solution.py:76
  60.9 0.1 pad_maximum_fusion
  61.0 0.1 dynamic-slice_bitcast_fusion.2
  61.1 0.1 collective-permute-start.10
  61.2 0.6 select_reduce_fusion.17
  62.5 1.2 %constant_dynamic-slice_fusion.2 = (f32[256,256]{1,0:T(8,128)S(1)}, f32[256,256]{1,0:T(8,128)S(1)}, f32[256,256]{1,0:T(8,128)S(1)}) fusion(f32[3840,256]{1,0:T(8,128)} %param.5, s32[]{:T(128)S(6)} %select_n.330, s32[]{:T(128)S(6)} %select_n.332, s32[]{:T(128)S(6)} %select_n.331), kind=kLoop, calls=%fused_computation.47 | loop fusion | bytes 1572876 | tf_op jit(solution)/shard_map/dynamic_slice | solution.py:42
  63.7 2.7 %collective-permute-start.6 = (f32[64,768]{1,0:T(8,128)S(1)}, f32[64,768]{1,0:T(8,128)S(1)}, u32[]{:S(2)}, u32[]{:S(2)}) collective-permute-start(f32[64,768]{1,0:T(8,128)S(1)} %get-tuple-element.38), channel_id=1, source_target_pairs={{0,1},{1,2},{2,3},{3,4},{4,5},{5,6},{6,7},{7,8},{8,9},{9,10},{10,1... | collective-permute-start | bytes 589832 | tf_op jit(solution)/shard_map/ppermute | solution.py:14
  66.4 1.2 %collective-permute-start.8 = (f32[64,768]{1,0:T(8,128)S(1)}, f32[64,768]{1,0:T(8,128)S(1)}, u32[]{:S(2)}, u32[]{:S(2)}) collective-permute-start(f32[64,768]{1,0:T(8,128)S(1)} %get-tuple-element.40), channel_id=1, source_target_pairs={{0,2},{1,3},{2,4},{3,5},{4,6},{5,7},{6,8},{7,9},{8,10},{9,11},{10,... | collective-permute-start | bytes 589832 | tf_op jit(solution)/shard_map/ppermute | solution.py:14
  67.6 3.3 %collective-permute-done.10 = f32[64,768]{1,0:T(8,128)S(1)} collective-permute-done((f32[64,768]{1,0:T(8,128)S(1)}, f32[64,768]{1,0:T(8,128)S(1)}, u32[]{:S(2)}, u32[]{:S(2)}) %collective-permute-start.10) | collective-permute-done | bytes 196640 | tf_op jit(solution)/shard_map/ppermute | solution.py:14
  70.9 1.9 %dynamic-slice_select_fusion.2 = (f32[64,256]{1,0:T(8,128)S(1)}, f32[64,256]{1,0:T(8,128)S(1)}, f32[64,256]{1,0:T(8,128)S(1)}) fusion(f32[64,768]{1,0:T(8,128)S(1)} %collective-permute-done.10, s32[]{:T(128)S(6)} %select_n.374, pred[]{:T(512)} %get-tuple-element.23, s32[]{:T(128)S(6)} %select_n.382, pred[]{:T(512)} %get-tuple-element.74, s32[]{:T(128)S(6)} %select_n.378, ...), kind=kLoop, calls=%fused_computation.35 | loop fusion | flops 49152 | bytes 393231 | tf_op jit(solution)/shard_map/jit(_where)/select_n | solution.py:52
  72.8 0.5 fusion.19
  73.3 10.6 %collective-permute-start.11 = (f32[64,256]{1,0:T(8,128)S(1)}, f32[64,256]{1,0:T(8,128)S(1)}, u32[]{:S(2)}, u32[]{:S(2)}) collective-permute-start(f32[64,256]{1,0:T(8,128)S(1)} %fusion.19), channel_id=1, source_target_pairs={{0,13},{1,14},{2,15},{3,0},{4,1},{5,2},{6,3},{7,4},{8,5},{9,6},{10... | collective-permute-start | bytes 196616 | tf_op jit(solution)/shard_map/ppermute | solution.py:14
  83.9 8.9 %collective-permute-done.8 = f32[64,768]{1,0:T(8,128)S(1)} collective-permute-done((f32[64,768]{1,0:T(8,128)S(1)}, f32[64,768]{1,0:T(8,128)S(1)}, u32[]{:S(2)}, u32[]{:S(2)}) %collective-permute-start.8) | collective-permute-done | bytes 196640 | tf_op jit(solution)/shard_map/ppermute | solution.py:14
  92.8 1.9 %dynamic-slice_select_fusion.5 = (f32[64,256]{1,0:T(8,128)S(1)}, f32[64,256]{1,0:T(8,128)S(1)}, f32[64,256]{1,0:T(8,128)S(1)}) fusion(f32[64,768]{1,0:T(8,128)S(1)} %collective-permute-done.8, s32[]{:T(128)S(6)} %select_n.357, pred[]{:T(512)} %get-tuple-element.17, s32[]{:T(128)S(6)} %select_n.365, pred[]{:T(512)} %get-tuple-element.70, s32[]{:T(128)S(6)} %select_n.361, ...), kind=kLoop, calls=%fused_computation.38 | loop fusion | flops 49152 | bytes 393231 | tf_op jit(solution)/shard_map/jit(_where)/select_n | solution.py:52
  94.7 0.5 fusion.13
  95.2 0.1 collective-permute-start.9
  95.3 1.9 %dynamic-slice_select_fusion.8 = (f32[64,256]{1,0:T(8,128)S(1)}, f32[64,256]{1,0:T(8,128)S(1)}, f32[64,256]{1,0:T(8,128)S(1)}) fusion(f32[64,768]{1,0:T(8,128)S(1)} %collective-permute-done.6, s32[]{:T(128)S(6)} %select_n.340, pred[]{:T(512)} %get-tuple-element.11, s32[]{:T(128)S(6)} %select_n.348, pred[]{:T(512)} %get-tuple-element.66, s32[]{:T(128)S(6)} %select_n.344, ...), kind=kLoop, calls=%fused_computation.41 | loop fusion | flops 49152 | bytes 393231 | tf_op jit(solution)/shard_map/jit(_where)/select_n | solution.py:52
  97.2 0.5 fusion.7
  97.7 5.7 %collective-permute-start.7 = (f32[64,256]{1,0:T(8,128)S(1)}, f32[64,256]{1,0:T(8,128)S(1)}, u32[]{:S(2)}, u32[]{:S(2)}) collective-permute-start(f32[64,256]{1,0:T(8,128)S(1)} %fusion.7), channel_id=1, source_target_pairs={{0,15},{1,0},{2,1},{3,2},{4,3},{5,4},{6,5},{7,6},{8,7},{9,8},{10,9... | collective-permute-start | bytes 196616 | tf_op jit(solution)/shard_map/ppermute | solution.py:14
  103.4 1.9 %select_bitcast_fusion.2 = (f32[64,256]{1,0:T(8,128)S(1)}, f32[64,256]{1,0:T(8,128)S(1)}, f32[64,256]{1,0:T(8,128)S(1)}) fusion(f32[4,64,768]{2,1,0:T(8,128)S(1)} %pad_maximum_fusion, s32[]{:T(128)S(6)} %select_n.312, s32[]{:T(128)S(6)} %select_n.315, pred[]{:T(512)} %get-tuple-element.5, s32[]{:T(128)S(6)} %select_n.327, pred[]{:T(512)} %get-tuple-element.62, ...), kind=kLoop, calls=%fused_computation.44 | loop fusion | flops 49152 | bytes 393235 | tf_op jit(solution)/shard_map/jit(_where)/select_n | solution.py:52
  105.4 1.1 %fusion.1 = f32[64,256]{1,0:T(8,128)} fusion(f32[64,256]{1,0:T(8,128)S(1)} %collective-permute-done.11, f32[64,256]{1,0:T(8,128)S(1)} %collective-permute-done.9, f32[64,256]{1,0:T(8,128)S(1)} %collective-permute-done.7, f32[64,256]{1,0:T(8,128)S(1)} %get-tuple-element.36, f32[64,256]{1,0:T(8,128)S(1)} %get-tuple-element.37, ...), kind=kOutput, calls=%fused_computation.2 | convolution fusion | flops 151535616 | bytes 1245184 | tf_op jit(solution)/shard_map/dot_general | solution.py:110
  (13 shorter events, 0.1 us)
Async XLA Ops:
  5.0 42.5 %collective-permute-start.2 = (f32[64,768]{1,0:T(8,128)S(1)}, f32[64,768]{1,0:T(8,128)S(1)}, u32[]{:S(2)}, u32[]{:S(2)}) collective-permute-start(f32[64,768]{1,0:T(8,128)S(1)} %pad_maximum_fusion.2), channel_id=1, source_target_pairs={{0,192},{16,208},{32,224},{48,240},{17,209},{33,225},{49,241},{65,... | collective-permute-start | bytes 589832 | tf_op jit(solution)/shard_map/ppermute | solution.py:66
  10.3 37.3 %collective-permute-start.1 = (f32[64,768]{1,0:T(8,128)S(1)}, f32[64,768]{1,0:T(8,128)S(1)}, u32[]{:S(2)}, u32[]{:S(2)}) collective-permute-start(f32[64,768]{1,0:T(8,128)S(1)} %pad_maximum_fusion.2), channel_id=1, source_target_pairs={{0,128},{16,144},{32,160},{48,176},{17,145},{33,161},{49,177},{65,... | collective-permute-start | bytes 589832 | tf_op jit(solution)/shard_map/ppermute | solution.py:66
  11.6 36.0 %collective-permute-start = (f32[64,768]{1,0:T(8,128)S(1)}, f32[64,768]{1,0:T(8,128)S(1)}, u32[]{:S(2)}, u32[]{:S(2)}) collective-permute-start(f32[64,768]{1,0:T(8,128)S(1)} %pad_maximum_fusion.2), channel_id=1, source_target_pairs={{0,64},{16,80},{32,96},{48,112},{17,81},{33,97},{49,113},{65,129},... | collective-permute-start | bytes 589832 | tf_op jit(solution)/shard_map/ppermute | solution.py:66
  47.6 9.3 %collective-permute-start.5 = (f32[64,768]{1,0:T(8,128)S(1)}, f32[64,768]{1,0:T(8,128)S(1)}, u32[]{:S(2)}, u32[]{:S(2)}) collective-permute-start(f32[64,768]{1,0:T(8,128)S(1)} %add_select_fusion), channel_id=1, source_target_pairs={{0,48},{16,32},{32,16},{48,0},{64,112},{80,96},{96,80},{112,64},{1... | collective-permute-start | bytes 589832 | tf_op jit(solution)/shard_map/ppermute | solution.py:76
  51.4 9.5 %collective-permute-start.4 = (f32[64,768]{1,0:T(8,128)S(1)}, f32[64,768]{1,0:T(8,128)S(1)}, u32[]{:S(2)}, u32[]{:S(2)}) collective-permute-start(f32[64,768]{1,0:T(8,128)S(1)} %add_select_fusion), channel_id=1, source_target_pairs={{0,32},{16,48},{32,0},{48,16},{64,96},{80,112},{96,64},{112,80},{1... | collective-permute-start | bytes 589832 | tf_op jit(solution)/shard_map/ppermute | solution.py:76
  51.5 9.4 %collective-permute-start.3 = (f32[64,768]{1,0:T(8,128)S(1)}, f32[64,768]{1,0:T(8,128)S(1)}, u32[]{:S(2)}, u32[]{:S(2)}) collective-permute-start(f32[64,768]{1,0:T(8,128)S(1)} %add_select_fusion), channel_id=1, source_target_pairs={{0,16},{16,0},{32,48},{48,32},{64,80},{80,64},{96,112},{112,96},{1... | collective-permute-start | bytes 589832 | tf_op jit(solution)/shard_map/ppermute | solution.py:76
  61.1 9.8 %collective-permute-start.10 = (f32[64,768]{1,0:T(8,128)S(1)}, f32[64,768]{1,0:T(8,128)S(1)}, u32[]{:S(2)}, u32[]{:S(2)}) collective-permute-start(f32[64,768]{1,0:T(8,128)S(1)} %get-tuple-element.39), channel_id=1, source_target_pairs={{0,3},{1,4},{2,5},{3,6},{4,7},{5,8},{6,9},{7,10},{8,11},{9,12},{10... | collective-permute-start | bytes 589832 | tf_op jit(solution)/shard_map/ppermute | solution.py:14
  63.7 31.6 %collective-permute-start.6 = (f32[64,768]{1,0:T(8,128)S(1)}, f32[64,768]{1,0:T(8,128)S(1)}, u32[]{:S(2)}, u32[]{:S(2)}) collective-permute-start(f32[64,768]{1,0:T(8,128)S(1)} %get-tuple-element.38), channel_id=1, source_target_pairs={{0,1},{1,2},{2,3},{3,4},{4,5},{5,6},{6,7},{7,8},{8,9},{9,10},{10,1... | collective-permute-start | bytes 589832 | tf_op jit(solution)/shard_map/ppermute | solution.py:14
  66.4 26.3 %collective-permute-start.8 = (f32[64,768]{1,0:T(8,128)S(1)}, f32[64,768]{1,0:T(8,128)S(1)}, u32[]{:S(2)}, u32[]{:S(2)}) collective-permute-start(f32[64,768]{1,0:T(8,128)S(1)} %get-tuple-element.40), channel_id=1, source_target_pairs={{0,2},{1,3},{2,4},{3,5},{4,6},{5,7},{6,8},{7,9},{8,10},{9,11},{10,... | collective-permute-start | bytes 589832 | tf_op jit(solution)/shard_map/ppermute | solution.py:14
  73.3 32.1 %collective-permute-start.11 = (f32[64,256]{1,0:T(8,128)S(1)}, f32[64,256]{1,0:T(8,128)S(1)}, u32[]{:S(2)}, u32[]{:S(2)}) collective-permute-start(f32[64,256]{1,0:T(8,128)S(1)} %fusion.19), channel_id=1, source_target_pairs={{0,13},{1,14},{2,15},{3,0},{4,1},{5,2},{6,3},{7,4},{8,5},{9,6},{10... | collective-permute-start | bytes 196616 | tf_op jit(solution)/shard_map/ppermute | solution.py:14
  95.2 10.2 %collective-permute-start.9 = (f32[64,256]{1,0:T(8,128)S(1)}, f32[64,256]{1,0:T(8,128)S(1)}, u32[]{:S(2)}, u32[]{:S(2)}) collective-permute-start(f32[64,256]{1,0:T(8,128)S(1)} %fusion.13), channel_id=1, source_target_pairs={{0,14},{1,15},{2,0},{3,1},{4,2},{5,3},{6,4},{7,5},{8,6},{9,7},{10,... | collective-permute-start | bytes 196616 | tf_op jit(solution)/shard_map/ppermute | solution.py:14
  97.7 7.7 %collective-permute-start.7 = (f32[64,256]{1,0:T(8,128)S(1)}, f32[64,256]{1,0:T(8,128)S(1)}, u32[]{:S(2)}, u32[]{:S(2)}) collective-permute-start(f32[64,256]{1,0:T(8,128)S(1)} %fusion.7), channel_id=1, source_target_pairs={{0,15},{1,0},{2,1},{3,2},{4,3},{5,4},{6,5},{7,6},{8,7},{9,8},{10,9... | collective-permute-start | bytes 196616 | tf_op jit(solution)/shard_map/ppermute | solution.py:14
